TPU v7x, 32 devices: a whole 2x2x4 slice. The times are simulated.
32 devices in a mesh: grp: 8 (over z, x), rep: 4 (over y, core).
Axes of the slice: x: 2, y: 2, z: 4, core: 2. Of those that a mesh axis runs over, the one named last changes fastest.
Arguments:
- three_center: bfloat16 [4, 64, 32, 6, 4096], P('rep', 'grp'), may hold values from -2 to 2
- metric: bfloat16 [4, 64, 64], P('rep'), may hold values from -0.75 to 0.75
- occupied: bfloat16 [2048, 48], replicated, may hold values from -0.3125 to 0.3125
- nu_list: int32 [32, 6], replicated, may hold values from 0 to 31, as said below
- nu_count: int32 [32], replicated, may hold values from 1 to 6
- block_size: int32 [32], replicated, may hold values from 32 to 64
Outputs:
- exchange_matrix: float32 [2048, 2048], P('rep', 'grp')
Inputs may be any that keep to these rules, and one draw needn't show every extreme that they name: `nu_list`: entry 0 of row m is m itself; the other entries of a row are distinct blocks other than m.
All inputs are finite; a program needn't handle non-finite values.
Results may differ from a plain program's by a relative error of at most 0.0024.
Values may be sent and summed in bfloat16 or wider, within the bound.
No kernel may reach another device: no remote copies, remote signals or barrier semaphores. Data moves between devices by JAX's collectives and lax.ppermute only.
A program may use at most 192 MiB of HBM per device.

v0:
```python
import jax
import jax.numpy as jnp
import numpy as np
from jax import lax
from jax.sharding import PartitionSpec as P

NB = 64


def snake(a_size, b_size):
    if a_size % 2:
        return [(a, b) for b, a in snake(b_size, a_size)]
    if b_size == 1:
        return [(a, 0) for a in range(a_size)]
    path = []
    for a in range(a_size):
        cols = (
            range(b_size)
            if a == 0
            else range(1, b_size) if a % 2 == 0 else range(b_size - 1, 0, -1)
        )
        path += [(a, b) for b in cols]
    path += [(a, 0) for a in range(a_size - 1, 0, -1)]
    return path


def ring_order(mesh):
    n = mesh.shape["grp"]
    try:
        devs = np.asarray(mesh.devices).reshape(n, -1)[:, 0]
        coords = [tuple(d.coords) for d in devs]
    except (AttributeError, TypeError):
        return list(range(n))
    varying = [i for i in range(len(coords[0])) if len({c[i] for c in coords}) > 1]
    if len(varying) == 1:
        key = sorted(range(n), key=lambda g: coords[g][varying[0]])
        return key
    if len(varying) != 2:
        return list(range(n))
    i, j = varying
    avals = sorted({c[i] for c in coords})
    bvals = sorted({c[j] for c in coords})
    where = {(avals.index(c[i]), bvals.index(c[j])): g for g, c in enumerate(coords)}
    if len(where) != n:
        return list(range(n))
    return [where[p] for p in snake(len(avals), len(bvals))]


def scatter_sum(term):
    n_rep = lax.axis_size("rep")
    if n_rep & n_rep - 1:
        return lax.psum_scatter(term, "rep", scatter_dimension=0, tiled=True)
    me = lax.axis_index("rep")
    bits = n_rep.bit_length() - 1
    per = term.shape[0] // n_rep
    buf = term.reshape((2,) * bits + (per,) + term.shape[1:])
    for b in range(bits):
        d = 1 << b
        axis = buf.ndim - 3
        mine = me // d % 2
        keep = lax.dynamic_index_in_dim(buf, mine, axis=axis, keepdims=False)
        send = lax.dynamic_index_in_dim(buf, 1 - mine, axis=axis, keepdims=False)
        got = lax.ppermute(send, "rep", [(i, i ^ d) for i in range(n_rep)])
        buf = keep + got
    return buf.reshape(per, term.shape[1])


def make_body(ring):
    n = len(ring)
    pos_of = np.zeros(n, np.int32)
    for p, g in enumerate(ring):
        pos_of[g] = p
    ring_arr = np.asarray(ring, np.int32)

    def shifted(s):
        return [(ring[p], ring[(p + s) % n]) for p in range(n)]

    def body(three_center, metric, occupied, nu_list, nu_count, block_size):
        n_mu, knu = nu_list.shape
        n_occ = occupied.shape[1]
        aux_dev = three_center.shape[1]
        lanes = jnp.arange(NB, dtype=jnp.int32)
        row_live = lanes[None, :] < block_size[:, None]
        col_live = lanes[None, None, :] < block_size[nu_list][:, :, None]
        slot_live = jnp.arange(knu, dtype=jnp.int32)[None, :] < nu_count[:, None]
        keep = col_live & slot_live[:, :, None]
        picked = occupied.reshape(n_mu, NB, n_occ)[nu_list]
        picked = jnp.where(keep[..., None], picked, jnp.zeros((), jnp.bfloat16))
        pair = 2
        blank = jnp.zeros_like(picked)
        weight = jnp.concatenate(
            [jnp.concatenate([picked, blank], axis=-1), jnp.concatenate([blank, picked], axis=-1)],
            axis=-2,
        )
        tiles = NB // pair
        tc = jnp.swapaxes(three_center[0], 1, 2).reshape(aux_dev, knu, n_mu, tiles, pair * NB)
        half = jnp.einsum("qkmtl,mklc->qmtc", tc, weight, preferred_element_type=jnp.float32)
        half = half.reshape(aux_dev, n_mu, NB, n_occ)
        half = jnp.where(row_live[None, :, :, None], half, 0.0).astype(jnp.bfloat16)
        mu_dev = n_mu // n
        n_split = 2 if mu_dev % 2 == 0 else 1
        mu_c = mu_dev // n_split
        half = half.reshape(aux_dev, n, mu_dev, NB * n_occ)
        me = lax.axis_index("grp")
        pos = jnp.asarray(pos_of)[me]
        ring_c = jnp.asarray(ring_arr)
        radius = n // 4
        helds = []
        for h in range(n_split):
            part = half[:, :, h * mu_c : (h + 1) * mu_c].reshape(aux_dev, n * mu_c, NB * n_occ)
            regrouped = lax.all_to_all(part, "grp", split_axis=1, concat_axis=0, tiled=True)
            n_aux = regrouped.shape[0]
            mixed = jnp.dot(
                metric[0], regrouped.reshape(n_aux, -1), preferred_element_type=jnp.float32
            )
            mixed = mixed.astype(jnp.bfloat16).reshape(n_aux, mu_c, NB, n_occ)
            orbital = jnp.transpose(mixed, (1, 2, 0, 3)).reshape(mu_c * NB, n_aux * n_occ)
            held = {0: orbital}
            fwd = orbital
            bwd = orbital
            for k in range(1, radius + 1):
                fwd = lax.ppermute(fwd, "grp", shifted(1))
                held[-k] = fwd
                bwd = lax.ppermute(bwd, "grp", shifted(-1))
                held[k] = bwd
            helds.append(held)
        held = {off: jnp.concatenate([hd[off] for hd in helds], axis=0) for off in helds[0]}
        rows = mu_dev * NB

        def start_of(off):
            return ring_c[(pos + off) % n] * rows

        def prod(xo, yo):
            return jnp.dot(held[xo], held[yo].T, preferred_element_type=jnp.float32)

        local = []
        outgoing = {}
        for d in range(n // 2 + 1):
            xo = -((d + 1) // 2)
            yo = xo + d
            blk = prod(xo, yo)
            s = d // 2
            if s == 0:
                local.append((-d, blk))
            else:
                outgoing.setdefault(s, []).append((-d, blk))
            if 0 < d < n // 2:
                outgoing.setdefault(xo, []).append((d, blk.T))
        placed = list(local)
        for s, items in sorted(outgoing.items()):
            stack = jnp.stack([b for _, b in items])
            got = lax.ppermute(stack, "grp", shifted(s))
            placed += [(off, got[i]) for i, (off, _) in enumerate(items)]
        term = jnp.zeros((n * rows, rows), jnp.float32)
        for off, blk in placed:
            term = lax.dynamic_update_slice_in_dim(term, blk, start_of(off), axis=0)
        return scatter_sum(term)

    return body


def solution(mesh):
    return jax.shard_map(
        make_body(ring_order(mesh)),
        mesh=mesh,
        in_specs=(P("rep", "grp", None, None, None), P("rep", None, None), P(), P(), P(), P()),
        out_specs=P("rep", "grp"),
        check_vma=False,
    )
```

profile of v0, /device:TPU:2, one launch (start us, length us, event | category | flops | bytes accessed | tf_op | source)
XLA Modules:
  0.0 207.9 jit_solution(4243646130246210751)
XLA Ops:
  0.0 0.7 compare_select_fusion
  0.9 1.3 reshape.104
  2.4 0.7 iota_compare_fusion.4
  3.2 1.6 gather_fusion
  4.7 1.0 gather_fusion.1
  5.9 7.4 %copy.30 = bf16[192,8,32,128]{3,2,1,0:T(8,128)(2,1)S(1)} copy(bf16[192,8,32,128]{3,1,2,0:T(8,128)(2,1)} %bitcast.112) | data formatting | bytes 25165824
  13.5 1.7 broadcast_select_fusion
  15.1 7.2 %fusion.14 = bf16[8,32,32,96]{3,2,0,1:T(8,128)(2,1)} fusion(bf16[8,6,32,32,128]{4,3,2,1,0:T(8,128)(2,1)S(1)} %bitcast.113, bf16[32,6,64,48]{2,3,1,0:T(8,128)(2,1)} %broadcast_select_fusion), kind=kOutput, calls=%fused_computation.20 | convolution fusion | flops 1226833920 | bytes 15335424 | tf_op jit(solution)/shard_map/qkmtl,mklc->qmtc/dot_general | solution.py:97
  22.3 4.2 %reshape.106 = bf16[8,8,4,3072]{3,0,2,1:T(8,128)(2,1)S(1)} reshape(bf16[8,32,32,96]{3,2,0,1:T(8,128)(2,1)} %fusion.14) | data formatting | bytes 3145728 | tf_op jit(solution)/shard_map/reshape | solution.py:98
  26.5 0.3 broadcast_in_dim.46
  26.8 0.7 broadcast_in_dim.47
  27.6 0.5 select_convert_fusion
  28.1 1.0 fusion.35
  29.1 25.8 %all_to_all.30 = bf16[8,16,3072]{2,0,1:T(8,128)(2,1)S(1)} all-to-all(bf16[8,16,3072]{2,0,1:T(8,128)(2,1)S(1)} %bitcast.120), channel_id=1, replica_groups=mesh['grp'=8,'rep'=4] {'grp'}, dimensions={1} | all-to-all | bytes 1572864 | tf_op jit(solution)/shard_map/all_to_all | solution.py:111
  55.0 4.2 %all-to-all-start.1 = ((bf16[8,16,3072]{2,0,1:T(8,128)(2,1)}), bf16[8,16,3072]{2,0,1:T(8,128)(2,1)S(1)}, u32[]{:S(2)}, u32[]{:S(2)}) async-start(bf16[8,16,3072]{2,0,1:T(8,128)(2,1)} %bitcast.15), calls=%async_computation.1 | async-start | bytes 1572864 | tf_op jit(solution)/shard_map/all_to_all | solution.py:111
  59.1 0.6 dynamic_slice.41
  66.3 0.7 fusion.36
  68.2 1.2 fusion.4
  69.5 3.3 %reshape.109 = bf16[64,2,64,48]{3,2,1,0:T(8,128)(2,1)S(1)} reshape(bf16[64,6144]{1,0:T(8,128)(2,1)} %fusion.4) | data formatting | bytes 1572864 | tf_op jit(solution)/shard_map/reshape | solution.py:116
  72.7 4.2 %copy.23 = bf16[2,64,64,48]{1,0,3,2:T(2,128)(2,1)} copy(bf16[2,64,64,48]{3,1,0,2:T(8,128)(2,1)S(1)} %bitcast.116) | data formatting | bytes 1572864 | tf_op jit(solution)/shard_map/transpose | solution.py:117
  77.0 3.9 %reshape.110 = bf16[128,3072]{0,1:T(8,128)(2,1)} reshape(bf16[2,64,64,48]{1,0,3,2:T(2,128)(2,1)} %copy.23) | data formatting | bytes 1572864 | tf_op jit(solution)/shard_map/reshape | solution.py:117
  80.9 2.0 collective-permute-start.4
  82.9 2.1 %constant_dynamic-update-slice_fusion.1 = bf16[256,3072]{0,1:T(8,128)(2,1)} fusion(bf16[128,3072]{0,1:T(8,128)(2,1)} %reshape.110), kind=kLoop, calls=%fused_computation.43 | loop fusion | bytes 1572864
  85.0 0.3 fusion.5
  85.4 2.2 %reshape.113 = bf16[64,2,64,48]{3,2,1,0:T(8,128)(2,1)S(1)} reshape(bf16[64,6144]{1,0:T(8,128)(2,1)S(1)} %fusion.5) | data formatting | bytes 1572864 | tf_op jit(solution)/shard_map/reshape | solution.py:116
  87.6 4.2 %copy.24 = bf16[2,64,64,48]{1,0,3,2:T(2,128)(2,1)} copy(bf16[2,64,64,48]{3,1,0,2:T(8,128)(2,1)S(1)} %bitcast.117) | data formatting | bytes 1572864 | tf_op jit(solution)/shard_map/transpose | solution.py:117
  91.8 3.1 %reshape.114 = bf16[128,3072]{0,1:T(8,128)(2,1)S(1)} reshape(bf16[2,64,64,48]{1,0,3,2:T(2,128)(2,1)} %copy.24) | data formatting | bytes 1572864 | tf_op jit(solution)/shard_map/reshape | solution.py:117
  95.1 2.0 collective-permute-start.5
  97.1 1.0 constant_dynamic-update-slice_fusion
  98.2 2.5 %convolution_dynamic-update-slice_fusion = f32[2048,256]{1,0:T(8,128)S(1)} fusion(f32[2048,256]{1,0:T(8,128)S(1)} %broadcast_in_dim.45, s32[]{:T(128)S(6)} %select_n.132, bf16[256,3072]{0,1:T(8,128)(2,1)} %constant_dynamic-update-slice_fusion), kind=kOutput, calls=%fused_computation.25 | convolution fusion | flops 402653184 | bytes 3407876 | tf_op jit(solution)/shard_map/dot_general | solution.py:134
  100.7 1.0 collective-permute-done
  101.7 1.3 constant_dynamic-update-slice_fusion.3
  103.0 1.3 constant_dynamic-update-slice_fusion.7
  104.2 12.2 %collective-permute-done.1 = bf16[128,3072]{0,1:T(8,128)(2,1)} collective-permute-done((bf16[128,3072]{0,1:T(8,128)(2,1)S(1)}, bf16[128,3072]{0,1:T(8,128)(2,1)}, u32[]{:S(2)}, u32[]{:S(2)}) %collective-permute-start.1) | collective-permute-done | bytes 786464 | tf_op jit(solution)/shard_map/ppermute | solution.py:122
  116.4 1.3 constant_dynamic-update-slice_fusion.2
  118.0 0.6 fusion.38
  118.6 2.0 constant_dynamic-update-slice_fusion.11
  120.7 0.4 collective-permute-start.2
  121.1 1.8 collective-permute-start.7
  122.9 0.3 collective-permute-start.3
  127.0 1.8 collective-permute-start.10
  128.8 1.5 collective-permute-start.9
  130.3 5.8 %collective-permute-done.7 = f32[2,256,256]{1,2,0:T(8,128)} collective-permute-done((f32[2,256,256]{1,2,0:T(8,128)S(1)}, f32[2,256,256]{1,2,0:T(8,128)}, u32[]{:S(2)}, u32[]{:S(2)}) %collective-permute-start.7) | collective-permute-done | bytes 524320 | tf_op jit(solution)/shard_map/ppermute | solution.py:152
  136.1 1.1 slice_bitcast_fusion.2
  137.5 4.1 %collective-permute-done.2 = bf16[128,3072]{0,1:T(8,128)(2,1)} collective-permute-done((bf16[128,3072]{0,1:T(8,128)(2,1)}, bf16[128,3072]{0,1:T(8,128)(2,1)}, u32[]{:S(2)}, u32[]{:S(2)}) %collective-permute-start.2) | collective-permute-done | bytes 786464 | tf_op jit(solution)/shard_map/ppermute | solution.py:122
  141.5 1.3 constant_dynamic-update-slice_fusion.5
  142.8 12.5 %collective-permute-done.3 = bf16[128,3072]{0,1:T(8,128)(2,1)} collective-permute-done((bf16[128,3072]{0,1:T(8,128)(2,1)}, bf16[128,3072]{0,1:T(8,128)(2,1)}, u32[]{:S(2)}, u32[]{:S(2)}) %collective-permute-start.3) | collective-permute-done | bytes 786464 | tf_op jit(solution)/shard_map/ppermute | solution.py:122
  155.4 1.3 constant_dynamic-update-slice_fusion.4
  156.7 0.6 fusion.37
  157.3 2.4 %collective-permute-start.6 = (f32[1,256,256]{1,2,0:T(8,128)S(1)}, f32[1,256,256]{1,2,0:T(8,128)S(1)}, u32[]{:S(2)}, u32[]{:S(2)}) collective-permute-start(f32[1,256,256]{1,2,0:T(8,128)S(1)} %bitcast.124), channel_id=1, source_target_pairs={{0,12},{8,4},{16,0},{24,8},{28,16},{20,24},{12,28},{4,20},{1,13},{... | collective-permute-start | bytes 786440 | tf_op jit(solution)/shard_map/ppermute | solution.py:152
  159.7 0.8 pad_maximum_fusion.1
  160.5 0.6 collective-permute-start.8
  161.1 7.4 %collective-permute-done.9 = bf16[128,3072]{0,1:T(8,128)(2,1)} collective-permute-done((bf16[128,3072]{0,1:T(8,128)(2,1)}, bf16[128,3072]{0,1:T(8,128)(2,1)}, u32[]{:S(2)}, u32[]{:S(2)}) %collective-permute-start.9) | collective-permute-done | bytes 786464 | tf_op jit(solution)/shard_map/ppermute | solution.py:124
  168.5 2.7 %fusion.23 = f32[1,256,256]{2,1,0:T(8,128)} fusion(bf16[256,3072]{0,1:T(8,128)(2,1)S(1)} %constant_dynamic-update-slice_fusion.4, bf16[128,3072]{0,1:T(8,128)(2,1)} %collective-permute-done.10, bf16[128,3072]{0,1:T(8,128)(2,1)} %collective-permute-done.9), kind=kOutput, calls=%fused_computation.26 | convolution fusion | flops 405798912 | bytes 3407872 | tf_op jit(solution)/shard_map/dot_general | solution.py:134
  171.2 7.8 %collective-permute-start.11 = (f32[1,256,256]{2,1,0:T(8,128)}, f32[1,256,256]{2,1,0:T(8,128)}, u32[]{:S(2)}, u32[]{:S(2)}) collective-permute-start(f32[1,256,256]{2,1,0:T(8,128)} %fusion.23), channel_id=1, source_target_pairs={{0,16},{8,24},{16,28},{24,20},{28,12},{20,4},{12,0},{4,8},{1,17},{... | collective-permute-start | bytes 786440 | tf_op jit(solution)/shard_map/ppermute | solution.py:152
  179.0 0.7 copy-done.5
  179.7 1.1 copy.25
  181.0 6.7 %collective-permute-done.11 = f32[1,256,256]{2,1,0:T(8,128)} collective-permute-done((f32[1,256,256]{2,1,0:T(8,128)}, f32[1,256,256]{2,1,0:T(8,128)}, u32[]{:S(2)}, u32[]{:S(2)}) %collective-permute-start.11) | collective-permute-done | bytes 262176 | tf_op jit(solution)/shard_map/ppermute | solution.py:152
  187.7 1.0 bitcast_dynamic-update-slice_fusion
  188.9 2.7 %collective-permute-done.12 = f32[2,512,256]{2,1,0:T(8,128)} collective-permute-done((f32[2,512,256]{2,1,0:T(8,128)S(1)}, f32[2,512,256]{2,1,0:T(8,128)}, u32[]{:S(2)}, u32[]{:S(2)}) %collective-permute-start.12) | collective-permute-done | bytes 1048608 | tf_op jit(solution)/shard_map/ppermute | solution.py:63
  191.6 1.4 bitcast_add_fusion
  193.1 1.6 collective-permute-start.13
  194.6 12.5 %collective-permute-done.13 = f32[512,256]{1,0:T(8,128)S(1)} collective-permute-done((f32[512,256]{1,0:T(8,128)S(1)}, f32[512,256]{1,0:T(8,128)S(1)}, u32[]{:S(2)}, u32[]{:S(2)}) %collective-permute-start.13) | collective-permute-done | bytes 524320 | tf_op jit(solution)/shard_map/ppermute | solution.py:63
  207.1 0.9 bitcast_add_fusion.1
  (45 shorter events, 1.8 us)
Async XLA Ops:
  0.0 68.2 %copy-start = (bf16[1,64,64]{2,1,0:T(8,128)(2,1)S(1)}, bf16[1,64,64]{2,1,0:T(8,128)(2,1)}, u32[]{:S(2)}) copy-start(bf16[1,64,64]{2,1,0:T(8,128)(2,1)} %param.9) | copy-start | bytes 24580
  0.0 3.2 %copy-start.1 = (s32[32]{0:T(128)S(1)}, s32[32]{0:T(128)}, u32[]{:S(2)}) copy-start(s32[32]{0:T(128)} %param.13) | copy-start | bytes 388
  4.7 1.1 copy-start.7
  29.1 30.0 %copy-start.8 = (s32[8]{0:T(128)S(1)}, s32[8]{0:T(128)}, u32[]{:S(2)}) copy-start(s32[8]{0:T(128)} %constant.133.clone) | copy-start | bytes 100
  29.1 37.2 %copy-start.6 = (s32[8]{0:T(128)S(1)}, s32[8]{0:T(128)}, u32[]{:S(2)}) copy-start(s32[8]{0:T(128)} %constant.134.clone) | copy-start | bytes 100
  55.0 30.1 %all-to-all-start.1 = ((bf16[8,16,3072]{2,0,1:T(8,128)(2,1)}), bf16[8,16,3072]{2,0,1:T(8,128)(2,1)S(1)}, u32[]{:S(2)}, u32[]{:S(2)}) async-start(bf16[8,16,3072]{2,0,1:T(8,128)(2,1)} %bitcast.15), calls=%async_computation.1 | async-start | bytes 1572864 | tf_op jit(solution)/shard_map/all_to_all | solution.py:111
  80.9 20.8 %collective-permute-start = (bf16[128,3072]{0,1:T(8,128)(2,1)}, bf16[128,3072]{0,1:T(8,128)(2,1)}, u32[]{:S(2)}, u32[]{:S(2)}) collective-permute-start(bf16[128,3072]{0,1:T(8,128)(2,1)} %reshape.110), channel_id=1, source_target_pairs={{0,8},{8,16},{16,24},{24,28},{28,20},{20,12},{12,4},{4,0},{1,9},{9... | collective-permute-start | bytes 2359304 | tf_op jit(solution)/shard_map/ppermute | solution.py:122
  80.9 22.1 %collective-permute-start.4 = (bf16[128,3072]{0,1:T(8,128)(2,1)}, bf16[128,3072]{0,1:T(8,128)(2,1)}, u32[]{:S(2)}, u32[]{:S(2)}) collective-permute-start(bf16[128,3072]{0,1:T(8,128)(2,1)} %reshape.110), channel_id=1, source_target_pairs={{0,4},{8,0},{16,8},{24,16},{28,24},{20,28},{12,20},{4,12},{1,5},{9... | collective-permute-start | bytes 2359304 | tf_op jit(solution)/shard_map/ppermute | solution.py:124
  95.0 21.4 %collective-permute-start.1 = (bf16[128,3072]{0,1:T(8,128)(2,1)S(1)}, bf16[128,3072]{0,1:T(8,128)(2,1)}, u32[]{:S(2)}, u32[]{:S(2)}) collective-permute-start(bf16[128,3072]{0,1:T(8,128)(2,1)S(1)} %reshape.114), channel_id=1, source_target_pairs={{0,8},{8,16},{16,24},{24,28},{28,20},{20,12},{12,4},{4,0},{1,9},{9... | collective-permute-start | bytes 2359304 | tf_op jit(solution)/shard_map/ppermute | solution.py:122
  95.1 22.7 %collective-permute-start.5 = (bf16[128,3072]{0,1:T(8,128)(2,1)S(1)}, bf16[128,3072]{0,1:T(8,128)(2,1)S(1)}, u32[]{:S(2)}, u32[]{:S(2)}) collective-permute-start(bf16[128,3072]{0,1:T(8,128)(2,1)S(1)} %reshape.114), channel_id=1, source_target_pairs={{0,4},{8,0},{16,8},{24,16},{28,24},{20,28},{12,20},{4,12},{1,5},{9... | collective-permute-start | bytes 2359304 | tf_op jit(solution)/shard_map/ppermute | solution.py:124
  117.8 0.9 copy-start.2
  118.0 2.7 %copy-start.3 = (bf16[256,3072]{0,1:T(8,128)(2,1)}, bf16[256,3072]{0,1:T(8,128)(2,1)S(1)}, u32[]{:S(2)}) copy-start(bf16[256,3072]{0,1:T(8,128)(2,1)S(1)} %constant_dynamic-update-slice_fusion.6) | copy-start | bytes 4718596
  120.7 20.8 %collective-permute-start.2 = (bf16[128,3072]{0,1:T(8,128)(2,1)}, bf16[128,3072]{0,1:T(8,128)(2,1)}, u32[]{:S(2)}, u32[]{:S(2)}) collective-permute-start(bf16[128,3072]{0,1:T(8,128)(2,1)} %collective-permute-done), channel_id=1, source_target_pairs={{0,8},{8,16},{16,24},{24,28},{28,20},{20,12},{12,4},{4,0},{1,9},{9... | collective-permute-start | bytes 2359304 | tf_op jit(solution)/shard_map/ppermute | solution.py:122
  121.1 15.0 %collective-permute-start.7 = (f32[2,256,256]{1,2,0:T(8,128)S(1)}, f32[2,256,256]{1,2,0:T(8,128)}, u32[]{:S(2)}, u32[]{:S(2)}) collective-permute-start(f32[2,256,256]{1,2,0:T(8,128)S(1)} %pad_maximum_fusion), channel_id=1, source_target_pairs={{0,4},{8,0},{16,8},{24,16},{28,24},{20,28},{12,20},{4,12},{1,5},{9... | collective-permute-start | bytes 1572872 | tf_op jit(solution)/shard_map/ppermute | solution.py:152
  122.9 32.5 %collective-permute-start.3 = (bf16[128,3072]{0,1:T(8,128)(2,1)}, bf16[128,3072]{0,1:T(8,128)(2,1)}, u32[]{:S(2)}, u32[]{:S(2)}) collective-permute-start(bf16[128,3072]{0,1:T(8,128)(2,1)} %collective-permute-done.1), channel_id=1, source_target_pairs={{0,8},{8,16},{16,24},{24,28},{28,20},{20,12},{12,4},{4,0},{1,9},{9... | collective-permute-start | bytes 2359304 | tf_op jit(solution)/shard_map/ppermute | solution.py:122
  127.0 34.1 %collective-permute-start.10 = (bf16[128,3072]{0,1:T(8,128)(2,1)}, bf16[128,3072]{0,1:T(8,128)(2,1)}, u32[]{:S(2)}, u32[]{:S(2)}) collective-permute-start(bf16[128,3072]{0,1:T(8,128)(2,1)} %copy-done.2), channel_id=1, source_target_pairs={{0,4},{8,0},{16,8},{24,16},{28,24},{20,28},{12,20},{4,12},{1,5},{9... | collective-permute-start | bytes 2359304 | tf_op jit(solution)/shard_map/ppermute | solution.py:124
  128.8 39.7 %collective-permute-start.9 = (bf16[128,3072]{0,1:T(8,128)(2,1)}, bf16[128,3072]{0,1:T(8,128)(2,1)}, u32[]{:S(2)}, u32[]{:S(2)}) collective-permute-start(bf16[128,3072]{0,1:T(8,128)(2,1)} %collective-permute-done.4), channel_id=1, source_target_pairs={{0,4},{8,0},{16,8},{24,16},{28,24},{20,28},{12,20},{4,12},{1,5},{9... | collective-permute-start | bytes 2359304 | tf_op jit(solution)/shard_map/ppermute | solution.py:124
  137.5 19.2 %copy-start.4 = (bf16[256,3072]{0,1:T(8,128)(2,1)S(1)}, bf16[256,3072]{0,1:T(8,128)(2,1)}, u32[]{:S(2)}) copy-start(bf16[256,3072]{0,1:T(8,128)(2,1)} %copy-done.3) | copy-start | bytes 4718596
  157.3 21.7 %collective-permute-start.6 = (f32[1,256,256]{1,2,0:T(8,128)S(1)}, f32[1,256,256]{1,2,0:T(8,128)S(1)}, u32[]{:S(2)}, u32[]{:S(2)}) collective-permute-start(f32[1,256,256]{1,2,0:T(8,128)S(1)} %bitcast.124), channel_id=1, source_target_pairs={{0,12},{8,4},{16,0},{24,8},{28,16},{20,24},{12,28},{4,20},{1,13},{... | collective-permute-start | bytes 786440 | tf_op jit(solution)/shard_map/ppermute | solution.py:152
  160.5 20.4 %collective-permute-start.8 = (f32[2,256,256]{2,1,0:T(8,128)}, f32[2,256,256]{2,1,0:T(8,128)S(1)}, u32[]{:S(2)}, u32[]{:S(2)}) collective-permute-start(f32[2,256,256]{2,1,0:T(8,128)} %pad_maximum_fusion.1), channel_id=1, source_target_pairs={{0,8},{8,16},{16,24},{24,28},{28,20},{20,12},{12,4},{4,0},{1,9},{9... | collective-permute-start | bytes 1572872 | tf_op jit(solution)/shard_map/ppermute | solution.py:152
  171.2 16.5 %collective-permute-start.11 = (f32[1,256,256]{2,1,0:T(8,128)}, f32[1,256,256]{2,1,0:T(8,128)}, u32[]{:S(2)}, u32[]{:S(2)}) collective-permute-start(f32[1,256,256]{2,1,0:T(8,128)} %fusion.23), channel_id=1, source_target_pairs={{0,16},{8,24},{16,28},{24,20},{28,12},{20,4},{12,0},{4,8},{1,17},{... | collective-permute-start | bytes 786440 | tf_op jit(solution)/shard_map/ppermute | solution.py:152
  179.0 0.7 copy-start.5
  188.8 2.9 %collective-permute-start.12 = (f32[2,512,256]{2,1,0:T(8,128)S(1)}, f32[2,512,256]{2,1,0:T(8,128)}, u32[]{:S(2)}, u32[]{:S(2)}) collective-permute-start(f32[2,512,256]{2,1,0:T(8,128)S(1)} %dynamic-slice_bitcast_fusion), channel_id=1, source_target_pairs={{0,1},{1,0},{2,3},{3,2},{4,5},{5,4},{6,7},{7,6},{8,9},{9,8},{10,11... | collective-permute-start | bytes 3145736 | tf_op jit(solution)/shard_map/ppermute | solution.py:63
  193.1 14.0 %collective-permute-start.13 = (f32[512,256]{1,0:T(8,128)S(1)}, f32[512,256]{1,0:T(8,128)S(1)}, u32[]{:S(2)}, u32[]{:S(2)}) collective-permute-start(f32[512,256]{1,0:T(8,128)S(1)} %dynamic-slice_bitcast_fusion.1), channel_id=1, source_target_pairs={{0,2},{1,3},{2,0},{3,1},{4,6},{5,7},{6,4},{7,5},{8,10},{9,11},{10,... | collective-permute-start | bytes 1572872 | tf_op jit(solution)/shard_map/ppermute | solution.py:63
where the time goes:
time: 209 us; the launch traced here: 208 us
  waiting for transfers between devices  65 us (31%)
  local copies, waits for them, and re-layouts  54.5 us (26%)
  starting transfers between devices  26.3 us (13%)
  blocking collectives  25.8 us (12%)
  matrix products  17.2 us (8%)
  between operations  12.1 us (6%)
  other arithmetic  6.92 us (3%)
    ppermute x4, waiting for transfers between devices, body(): fwd = lax.ppermute(fwd, 'grp', shifted(1))  29.8 us
    all_to_all x1, blocking collectives, body(): lax.all_to_all(part, 'grp', split_axis=1, concat_axis=0, tiled=True)  25.8 us
    ppermute x2, waiting for transfers between devices, scatter_sum(): got = lax.ppermute(send, 'rep', [(i, i ^ d) for i in range(n_rep)])  15.2 us
    unnamed x23, local copies, waits for them, and re-layouts  14.1 us
    ppermute x4, waiting for transfers between devices, body(): got = lax.ppermute(stack, 'grp', shifted(s))  12.6 us
    ppermute x4, starting transfers between devices, body(): got = lax.ppermute(stack, 'grp', shifted(s))  12.5 us
    transpose x2, local copies, waits for them, and re-layouts, body(): jnp.transpose(mixed, (1, 2, 0, 3)).reshape(mu_c * NB, n_aux * n_occ)  8.5 us
    dot_general x5, matrix products, prod(): return jnp.dot(held[xo], held[yo].T, preferred_element_type=jnp.float32)  8.43 us
  transfers between devices with their start and end apart: 15, of which 9 were waited for; matrix products, arithmetic and copies ran while one was open for 21% of the time, Pallas kernels for 0%

commit v1 on v0

--- a/solution.py
+++ b/solution.py
@@ -108,7 +108,10 @@
         helds = []
         for h in range(n_split):
             part = half[:, :, h * mu_c : (h + 1) * mu_c].reshape(aux_dev, n * mu_c, NB * n_occ)
-            regrouped = lax.all_to_all(part, "grp", split_axis=1, concat_axis=0, tiled=True)
+            count = lax.axis_size("grp")
+            shards = jnp.stack(jnp.split(part, count, axis=1), axis=0)
+            shards = lax.all_to_all(shards, "grp", split_axis=0, concat_axis=0)
+            regrouped = jnp.concatenate(shards, axis=0)
             n_aux = regrouped.shape[0]
             mixed = jnp.dot(
                 metric[0], regrouped.reshape(n_aux, -1), preferred_element_type=jnp.float32

time: 209 us -> 217 us (1.038)
  blocking collectives: 25.8 us -> 0 us
  waiting for transfers between devices: 65 us -> 89.5 us
  starting transfers between devices: 26.3 us -> 32.9 us
  local copies, waits for them, and re-layouts: 54.5 us -> 59.6 us
  matrix products: 17.2 us -> 14.7 us
    all_to_all x1 -> x0, blocking collectives: 25.8 us -> none  [body(): lax.all_to_all(part, 'grp', split_axis=1, concat_axis=0, tiled=True)]
    all_to_all x1 -> x2, waiting for transfers between devices: 0.01 us -> 18.5 us  [body(): shards = lax.all_to_all(shards, 'grp', split_axis=0, concat_axis=0)]
    ppermute x4, waiting for transfers between devices: 7.43 us -> 25.2 us  [body(): bwd = lax.ppermute(bwd, 'grp', shifted(-1))]
    ppermute x4, waiting for transfers between devices: 29.8 us -> 17.8 us  [body(): fwd = lax.ppermute(fwd, 'grp', shifted(1))]
    all_to_all x1 -> x2, starting transfers between devices: 4.15 us -> 10.7 us  [body(): shards = lax.all_to_all(shards, 'grp', split_axis=0, concat_axis=0)]
    dot_general x5, matrix products: 8.43 us -> 5.13 us  [prod(): return jnp.dot(held[xo], held[yo].T, preferred_element_type=jnp.float32)]
    unnamed x23 -> x39, local copies, waits for them, and re-layouts: 14.1 us -> 16.3 us
  transfers between devices with their start and end apart: 15 -> 16, of which waited for: 9 -> 10; matrix products, arithmetic and copies ran while one was open for 21% -> 19% of each run, Pallas kernels for 0% -> 0%
where the time goes in v1:
time: 217 us; the launch traced here: 216 us
  waiting for transfers between devices  89.5 us (41%)
  local copies, waits for them, and re-layouts  59.6 us (27%)
  starting transfers between devices  32.9 us (15%)
  matrix products  14.7 us (7%)
  between operations  12.1 us (6%)
  other arithmetic  6.9 us (3%)
    ppermute x4, waiting for transfers between devices, body(): bwd = lax.ppermute(bwd, 'grp', shifted(-1))  25.2 us
    all_to_all x2, waiting for transfers between devices, body(): shards = lax.all_to_all(shards, 'grp', split_axis=0, concat_axis=0)  18.5 us
    ppermute x4, waiting for transfers between devices, body(): fwd = lax.ppermute(fwd, 'grp', shifted(1))  17.8 us
    unnamed x39, local copies, waits for them, and re-layouts  16.3 us
    ppermute x2, waiting for transfers between devices, scatter_sum(): got = lax.ppermute(send, 'rep', [(i, i ^ d) for i in range(n_rep)])  15.2 us
    ppermute x4, waiting for transfers between devices, body(): got = lax.ppermute(stack, 'grp', shifted(s))  12.8 us
    ppermute x4, starting transfers between devices, body(): got = lax.ppermute(stack, 'grp', shifted(s))  12.3 us
    all_to_all x2, starting transfers between devices, body(): shards = lax.all_to_all(shards, 'grp', split_axis=0, concat_axis=0)  10.7 us
  transfers between devices with their start and end apart: 16, of which 10 were waited for; matrix products, arithmetic and copies ran while one was open for 19% of the time, Pallas kernels for 0%

profile of v1, /device:TPU:2, one launch (start us, length us, event | category | flops | bytes accessed | tf_op | source)
XLA Modules:
  0.0 215.9 jit_solution(6538772136948504101)
XLA Ops:
  0.0 0.7 compare_select_fusion
  0.9 1.3 reshape.96
  2.4 0.7 iota_compare_fusion.4
  3.2 1.6 gather_fusion
  4.7 1.0 gather_fusion.1
  5.9 7.4 %copy.30 = bf16[192,8,32,128]{3,2,1,0:T(8,128)(2,1)S(1)} copy(bf16[192,8,32,128]{3,1,2,0:T(8,128)(2,1)} %bitcast.168) | data formatting | bytes 25165824
  13.5 1.6 broadcast_select_fusion
  15.1 7.1 %fusion.14 = bf16[8,32,32,96]{3,2,0,1:T(8,128)(2,1)} fusion(bf16[8,6,32,32,128]{4,3,2,1,0:T(8,128)(2,1)S(1)} %bitcast.169, bf16[32,6,64,48]{2,3,1,0:T(8,128)(2,1)} %broadcast_select_fusion), kind=kOutput, calls=%fused_computation.20 | convolution fusion | flops 1226833920 | bytes 15335424 | tf_op jit(solution)/shard_map/qkmtl,mklc->qmtc/dot_general | solution.py:97
  22.2 4.2 %reshape.98 = bf16[8,8,4,3072]{3,0,2,1:T(8,128)(2,1)S(1)} reshape(bf16[8,32,32,96]{3,2,0,1:T(8,128)(2,1)} %fusion.14) | data formatting | bytes 3145728 | tf_op jit(solution)/shard_map/reshape | solution.py:98
  26.8 0.7 broadcast_in_dim.47
  28.1 0.6 fusion.36
  28.8 0.6 fusion.35
  29.4 0.6 fusion.34
  30.1 0.6 fusion.33
  30.7 0.7 fusion.32
  31.4 0.6 fusion.31
  32.0 0.6 fusion.30
  32.6 0.6 fusion.29
  33.3 6.5 %all-to-all-start.1 = ((bf16[8,8,2,3072]{3,1,2,0:T(8,128)(2,1)}), bf16[8,8,2,3072]{3,1,2,0:T(8,128)(2,1)S(1)}, u32[]{:S(2)}, u32[]{:S(2)}) async-start(bf16[8,8,2,3072]{3,1,2,0:T(8,128)(2,1)} %fusion.29), calls=%async_computation.1 | async-start | bytes 1572864 | tf_op jit(solution)/shard_map/all_to_all | solution.py:113
  39.9 0.9 copy-done.2
  40.8 18.5 %all-to-all-done.1 = bf16[8,8,2,3072]{3,1,2,0:T(8,128)(2,1)S(1)} async-done(((bf16[8,8,2,3072]{3,1,2,0:T(8,128)(2,1)}), bf16[8,8,2,3072]{3,1,2,0:T(8,128)(2,1)S(1)}, u32[]{:S(2)}, u32[]{:S(2)}) %all-to-all-start.1) | async-done | bytes 786464 | tf_op jit(solution)/shard_map/all_to_all | solution.py:113
  59.3 4.2 %all-to-all-start = ((bf16[8,8,2,3072]{3,1,2,0:T(8,128)(2,1)}), bf16[8,8,2,3072]{3,1,2,0:T(8,128)(2,1)S(1)}, u32[]{:S(2)}, u32[]{:S(2)}) async-start(bf16[8,8,2,3072]{3,1,2,0:T(8,128)(2,1)} %copy-done.2), calls=%async_computation | async-start | bytes 1572864 | tf_op jit(solution)/shard_map/all_to_all | solution.py:113
  70.7 0.7 fusion.52
  72.7 1.2 fusion.5
  73.9 3.3 %reshape.103 = bf16[64,2,64,48]{3,2,1,0:T(8,128)(2,1)S(1)} reshape(bf16[64,6144]{1,0:T(8,128)(2,1)} %fusion.5) | data formatting | bytes 1572864 | tf_op jit(solution)/shard_map/reshape | solution.py:119
  77.2 4.3 %copy.24 = bf16[2,64,64,48]{1,0,3,2:T(2,128)(2,1)} copy(bf16[2,64,64,48]{3,1,0,2:T(8,128)(2,1)S(1)} %bitcast.172) | data formatting | bytes 1572864 | tf_op jit(solution)/shard_map/transpose | solution.py:120
  81.5 3.9 %reshape.104 = bf16[128,3072]{0,1:T(8,128)(2,1)} reshape(bf16[2,64,64,48]{1,0,3,2:T(2,128)(2,1)} %copy.24) | data formatting | bytes 1572864 | tf_op jit(solution)/shard_map/reshape | solution.py:120
  85.3 1.5 collective-permute-start.5
  87.4 1.2 fusion.4
  88.6 3.3 %reshape.100 = bf16[64,2,64,48]{3,2,1,0:T(8,128)(2,1)S(1)} reshape(bf16[64,6144]{1,0:T(8,128)(2,1)} %fusion.4) | data formatting | bytes 1572864 | tf_op jit(solution)/shard_map/reshape | solution.py:119
  91.9 4.3 %copy.23 = bf16[2,64,64,48]{1,0,3,2:T(2,128)(2,1)} copy(bf16[2,64,64,48]{3,1,0,2:T(8,128)(2,1)S(1)} %bitcast.173) | data formatting | bytes 1572864 | tf_op jit(solution)/shard_map/transpose | solution.py:120
  96.1 3.1 %reshape.101 = bf16[128,3072]{0,1:T(8,128)(2,1)S(1)} reshape(bf16[2,64,64,48]{1,0,3,2:T(2,128)(2,1)} %copy.23) | data formatting | bytes 1572864 | tf_op jit(solution)/shard_map/reshape | solution.py:120
  99.3 1.5 collective-permute-start.4
  101.5 1.3 constant_dynamic-update-slice_fusion
  102.9 0.6 convolution_dynamic-update-slice_fusion
  103.6 17.7 %collective-permute-done.4 = bf16[128,3072]{0,1:T(8,128)(2,1)S(1)} collective-permute-done((bf16[128,3072]{0,1:T(8,128)(2,1)S(1)}, bf16[128,3072]{0,1:T(8,128)(2,1)S(1)}, u32[]{:S(2)}, u32[]{:S(2)}) %collective-permute-start.4) | collective-permute-done | bytes 786464 | tf_op jit(solution)/shard_map/ppermute | solution.py:127
  121.4 1.1 collective-permute-done
  122.6 1.3 constant_dynamic-update-slice_fusion.3
  123.9 1.3 constant_dynamic-update-slice_fusion.6
  125.2 1.9 constant_dynamic-update-slice_fusion.2
  127.7 0.6 constant_dynamic-update-slice_fusion.11
  129.0 1.5 collective-permute-start.7
  134.9 1.5 collective-permute-start.10
  136.4 1.5 collective-permute-start.9
  137.8 6.2 %collective-permute-done.7 = f32[2,256,256]{1,2,0:T(8,128)} collective-permute-done((f32[2,256,256]{1,2,0:T(8,128)S(1)}, f32[2,256,256]{1,2,0:T(8,128)}, u32[]{:S(2)}, u32[]{:S(2)}) %collective-permute-start.7) | collective-permute-done | bytes 524320 | tf_op jit(solution)/shard_map/ppermute | solution.py:155
  144.0 1.1 slice_bitcast_fusion.2
  145.4 3.8 %collective-permute-done.2 = bf16[128,3072]{0,1:T(8,128)(2,1)} collective-permute-done((bf16[128,3072]{0,1:T(8,128)(2,1)}, bf16[128,3072]{0,1:T(8,128)(2,1)}, u32[]{:S(2)}, u32[]{:S(2)}) %collective-permute-start.2) | collective-permute-done | bytes 786464 | tf_op jit(solution)/shard_map/ppermute | solution.py:125
  149.2 1.3 constant_dynamic-update-slice_fusion.5
  150.5 12.8 %collective-permute-done.3 = bf16[128,3072]{0,1:T(8,128)(2,1)} collective-permute-done((bf16[128,3072]{0,1:T(8,128)(2,1)}, bf16[128,3072]{0,1:T(8,128)(2,1)}, u32[]{:S(2)}, u32[]{:S(2)}) %collective-permute-start.3) | collective-permute-done | bytes 786464 | tf_op jit(solution)/shard_map/ppermute | solution.py:125
  163.3 1.3 constant_dynamic-update-slice_fusion.4
  165.2 0.8 pad_maximum_fusion.1
  166.6 2.4 %collective-permute-start.6 = (f32[1,256,256]{1,2,0:T(8,128)S(1)}, f32[1,256,256]{1,2,0:T(8,128)S(1)}, u32[]{:S(2)}, u32[]{:S(2)}) collective-permute-start(f32[1,256,256]{1,2,0:T(8,128)S(1)} %bitcast.196), channel_id=1, source_target_pairs={{0,12},{8,4},{16,0},{24,8},{28,16},{20,24},{12,28},{4,20},{1,13},{... | collective-permute-start | bytes 786440 | tf_op jit(solution)/shard_map/ppermute | solution.py:155
  169.0 7.5 %collective-permute-done.9 = bf16[128,3072]{0,1:T(8,128)(2,1)} collective-permute-done((bf16[128,3072]{0,1:T(8,128)(2,1)}, bf16[128,3072]{0,1:T(8,128)(2,1)}, u32[]{:S(2)}, u32[]{:S(2)}) %collective-permute-start.9) | collective-permute-done | bytes 786464 | tf_op jit(solution)/shard_map/ppermute | solution.py:127
  176.5 2.7 %fusion.23 = f32[1,256,256]{2,1,0:T(8,128)} fusion(bf16[256,3072]{0,1:T(8,128)(2,1)S(1)} %constant_dynamic-update-slice_fusion.4, bf16[128,3072]{0,1:T(8,128)(2,1)} %collective-permute-done.10, bf16[128,3072]{0,1:T(8,128)(2,1)} %collective-permute-done.9), kind=kOutput, calls=%fused_computation.26 | convolution fusion | flops 405798912 | bytes 3407872 | tf_op jit(solution)/shard_map/dot_general | solution.py:137
  179.2 7.9 %collective-permute-start.11 = (f32[1,256,256]{2,1,0:T(8,128)}, f32[1,256,256]{2,1,0:T(8,128)}, u32[]{:S(2)}, u32[]{:S(2)}) collective-permute-start(f32[1,256,256]{2,1,0:T(8,128)} %fusion.23), channel_id=1, source_target_pairs={{0,16},{8,24},{16,28},{24,20},{28,12},{20,4},{12,0},{4,8},{1,17},{... | collective-permute-start | bytes 786440 | tf_op jit(solution)/shard_map/ppermute | solution.py:155
  187.1 0.7 copy-done.6
  187.8 1.1 copy.25
  189.1 6.6 %collective-permute-done.11 = f32[1,256,256]{2,1,0:T(8,128)} collective-permute-done((f32[1,256,256]{2,1,0:T(8,128)}, f32[1,256,256]{2,1,0:T(8,128)}, u32[]{:S(2)}, u32[]{:S(2)}) %collective-permute-start.11) | collective-permute-done | bytes 262176 | tf_op jit(solution)/shard_map/ppermute | solution.py:155
  195.6 1.0 bitcast_dynamic-update-slice_fusion
  196.8 2.7 %collective-permute-done.12 = f32[2,512,256]{2,1,0:T(8,128)} collective-permute-done((f32[2,512,256]{2,1,0:T(8,128)S(1)}, f32[2,512,256]{2,1,0:T(8,128)}, u32[]{:S(2)}, u32[]{:S(2)}) %collective-permute-start.12) | collective-permute-done | bytes 1048608 | tf_op jit(solution)/shard_map/ppermute | solution.py:63
  199.5 1.4 bitcast_add_fusion
  201.0 1.6 collective-permute-start.13
  202.5 12.4 %collective-permute-done.13 = f32[512,256]{1,0:T(8,128)S(1)} collective-permute-done((f32[512,256]{1,0:T(8,128)S(1)}, f32[512,256]{1,0:T(8,128)S(1)}, u32[]{:S(2)}, u32[]{:S(2)}) %collective-permute-start.13) | collective-permute-done | bytes 524320 | tf_op jit(solution)/shard_map/ppermute | solution.py:63
  215.0 0.9 bitcast_add_fusion.1
  (64 shorter events, 7.4 us)
Async XLA Ops:
  0.0 72.7 %copy-start = (bf16[1,64,64]{2,1,0:T(8,128)(2,1)S(1)}, bf16[1,64,64]{2,1,0:T(8,128)(2,1)}, u32[]{:S(2)}) copy-start(bf16[1,64,64]{2,1,0:T(8,128)(2,1)} %param.9) | copy-start | bytes 24580
  0.0 3.2 %copy-start.1 = (s32[32]{0:T(128)S(1)}, s32[32]{0:T(128)}, u32[]{:S(2)}) copy-start(s32[32]{0:T(128)} %param.13) | copy-start | bytes 388
  4.7 1.1 copy-start.8
  33.3 30.2 %copy-start.9 = (s32[8]{0:T(128)S(1)}, s32[8]{0:T(128)}, u32[]{:S(2)}) copy-start(s32[8]{0:T(128)} %constant.133.clone) | copy-start | bytes 100
  33.3 37.4 %copy-start.7 = (s32[8]{0:T(128)S(1)}, s32[8]{0:T(128)}, u32[]{:S(2)}) copy-start(s32[8]{0:T(128)} %constant.134.clone) | copy-start | bytes 100
  33.3 26.0 %all-to-all-start.1 = ((bf16[8,8,2,3072]{3,1,2,0:T(8,128)(2,1)}), bf16[8,8,2,3072]{3,1,2,0:T(8,128)(2,1)S(1)}, u32[]{:S(2)}, u32[]{:S(2)}) async-start(bf16[8,8,2,3072]{3,1,2,0:T(8,128)(2,1)} %fusion.29), calls=%async_computation.1 | async-start | bytes 1572864 | tf_op jit(solution)/shard_map/all_to_all | solution.py:113
  39.9 0.9 copy-start.2
  59.3 28.1 %all-to-all-start = ((bf16[8,8,2,3072]{3,1,2,0:T(8,128)(2,1)}), bf16[8,8,2,3072]{3,1,2,0:T(8,128)(2,1)S(1)}, u32[]{:S(2)}, u32[]{:S(2)}) async-start(bf16[8,8,2,3072]{3,1,2,0:T(8,128)(2,1)} %copy-done.2), calls=%async_computation | async-start | bytes 1572864 | tf_op jit(solution)/shard_map/all_to_all | solution.py:113
  85.3 38.5 %collective-permute-start.5 = (bf16[128,3072]{0,1:T(8,128)(2,1)}, bf16[128,3072]{0,1:T(8,128)(2,1)}, u32[]{:S(2)}, u32[]{:S(2)}) collective-permute-start(bf16[128,3072]{0,1:T(8,128)(2,1)} %reshape.104), channel_id=1, source_target_pairs={{0,4},{8,0},{16,8},{24,16},{28,24},{20,28},{12,20},{4,12},{1,5},{9... | collective-permute-start | bytes 2359304 | tf_op jit(solution)/shard_map/ppermute | solution.py:127
  86.8 38.4 %collective-permute-start.1 = (bf16[128,3072]{0,1:T(8,128)(2,1)}, bf16[128,3072]{0,1:T(8,128)(2,1)}, u32[]{:S(2)}, u32[]{:S(2)}) collective-permute-start(bf16[128,3072]{0,1:T(8,128)(2,1)} %reshape.104), channel_id=1, source_target_pairs={{0,8},{8,16},{16,24},{24,28},{28,20},{20,12},{12,4},{4,0},{1,9},{9... | collective-permute-start | bytes 2359304 | tf_op jit(solution)/shard_map/ppermute | solution.py:125
  99.3 22.0 %collective-permute-start.4 = (bf16[128,3072]{0,1:T(8,128)(2,1)S(1)}, bf16[128,3072]{0,1:T(8,128)(2,1)S(1)}, u32[]{:S(2)}, u32[]{:S(2)}) collective-permute-start(bf16[128,3072]{0,1:T(8,128)(2,1)S(1)} %reshape.101), channel_id=1, source_target_pairs={{0,4},{8,0},{16,8},{24,16},{28,24},{20,28},{12,20},{4,12},{1,5},{9... | collective-permute-start | bytes 2359304 | tf_op jit(solution)/shard_map/ppermute | solution.py:127
  100.8 21.8 %collective-permute-start = (bf16[128,3072]{0,1:T(8,128)(2,1)S(1)}, bf16[128,3072]{0,1:T(8,128)(2,1)}, u32[]{:S(2)}, u32[]{:S(2)}) collective-permute-start(bf16[128,3072]{0,1:T(8,128)(2,1)S(1)} %reshape.101), channel_id=1, source_target_pairs={{0,8},{8,16},{16,24},{24,28},{28,20},{20,12},{12,4},{4,0},{1,9},{9... | collective-permute-start | bytes 2359304 | tf_op jit(solution)/shard_map/ppermute | solution.py:125
  121.3 7.1 %copy-start.3 = (bf16[128,3072]{0,1:T(8,128)(2,1)}, bf16[128,3072]{0,1:T(8,128)(2,1)S(1)}, u32[]{:S(2)}) copy-start(bf16[128,3072]{0,1:T(8,128)(2,1)S(1)} %collective-permute-done.4) | copy-start | bytes 2359300
  125.2 2.5 %copy-start.4 = (bf16[256,3072]{0,1:T(8,128)(2,1)}, bf16[256,3072]{0,1:T(8,128)(2,1)S(1)}, u32[]{:S(2)}) copy-start(bf16[256,3072]{0,1:T(8,128)(2,1)S(1)} %constant_dynamic-update-slice_fusion.6) | copy-start | bytes 4718596
  128.4 20.8 %collective-permute-start.2 = (bf16[128,3072]{0,1:T(8,128)(2,1)}, bf16[128,3072]{0,1:T(8,128)(2,1)}, u32[]{:S(2)}, u32[]{:S(2)}) collective-permute-start(bf16[128,3072]{0,1:T(8,128)(2,1)} %collective-permute-done), channel_id=1, source_target_pairs={{0,8},{8,16},{16,24},{24,28},{28,20},{20,12},{12,4},{4,0},{1,9},{9... | collective-permute-start | bytes 2359304 | tf_op jit(solution)/shard_map/ppermute | solution.py:125
  129.0 15.0 %collective-permute-start.7 = (f32[2,256,256]{1,2,0:T(8,128)S(1)}, f32[2,256,256]{1,2,0:T(8,128)}, u32[]{:S(2)}, u32[]{:S(2)}) collective-permute-start(f32[2,256,256]{1,2,0:T(8,128)S(1)} %pad_maximum_fusion), channel_id=1, source_target_pairs={{0,4},{8,0},{16,8},{24,16},{28,24},{20,28},{12,20},{4,12},{1,5},{9... | collective-permute-start | bytes 1572872 | tf_op jit(solution)/shard_map/ppermute | solution.py:155
  130.5 32.7 %collective-permute-start.3 = (bf16[128,3072]{0,1:T(8,128)(2,1)}, bf16[128,3072]{0,1:T(8,128)(2,1)}, u32[]{:S(2)}, u32[]{:S(2)}) collective-permute-start(bf16[128,3072]{0,1:T(8,128)(2,1)} %collective-permute-done.1), channel_id=1, source_target_pairs={{0,8},{8,16},{16,24},{24,28},{28,20},{20,12},{12,4},{4,0},{1,9},{9... | collective-permute-start | bytes 2359304 | tf_op jit(solution)/shard_map/ppermute | solution.py:125
  134.9 34.1 %collective-permute-start.10 = (bf16[128,3072]{0,1:T(8,128)(2,1)}, bf16[128,3072]{0,1:T(8,128)(2,1)}, u32[]{:S(2)}, u32[]{:S(2)}) collective-permute-start(bf16[128,3072]{0,1:T(8,128)(2,1)} %collective-permute-done.5), channel_id=1, source_target_pairs={{0,4},{8,0},{16,8},{24,16},{28,24},{20,28},{12,20},{4,12},{1,5},{9... | collective-permute-start | bytes 2359304 | tf_op jit(solution)/shard_map/ppermute | solution.py:127
  136.4 40.1 %collective-permute-start.9 = (bf16[128,3072]{0,1:T(8,128)(2,1)}, bf16[128,3072]{0,1:T(8,128)(2,1)}, u32[]{:S(2)}, u32[]{:S(2)}) collective-permute-start(bf16[128,3072]{0,1:T(8,128)(2,1)} %copy-done.3), channel_id=1, source_target_pairs={{0,4},{8,0},{16,8},{24,16},{28,24},{20,28},{12,20},{4,12},{1,5},{9... | collective-permute-start | bytes 2359304 | tf_op jit(solution)/shard_map/ppermute | solution.py:127
  145.4 19.2 %copy-start.5 = (bf16[256,3072]{0,1:T(8,128)(2,1)S(1)}, bf16[256,3072]{0,1:T(8,128)(2,1)}, u32[]{:S(2)}) copy-start(bf16[256,3072]{0,1:T(8,128)(2,1)} %copy-done.4) | copy-start | bytes 4718596
  166.1 22.9 %collective-permute-start.8 = (f32[2,256,256]{2,1,0:T(8,128)}, f32[2,256,256]{2,1,0:T(8,128)S(1)}, u32[]{:S(2)}, u32[]{:S(2)}) collective-permute-start(f32[2,256,256]{2,1,0:T(8,128)} %pad_maximum_fusion.1), channel_id=1, source_target_pairs={{0,8},{8,16},{16,24},{24,28},{28,20},{20,12},{12,4},{4,0},{1,9},{9... | collective-permute-start | bytes 1572872 | tf_op jit(solution)/shard_map/ppermute | solution.py:155
  166.6 20.4 %collective-permute-start.6 = (f32[1,256,256]{1,2,0:T(8,128)S(1)}, f32[1,256,256]{1,2,0:T(8,128)S(1)}, u32[]{:S(2)}, u32[]{:S(2)}) collective-permute-start(f32[1,256,256]{1,2,0:T(8,128)S(1)} %bitcast.196), channel_id=1, source_target_pairs={{0,12},{8,4},{16,0},{24,8},{28,16},{20,24},{12,28},{4,20},{1,13},{... | collective-permute-start | bytes 786440 | tf_op jit(solution)/shard_map/ppermute | solution.py:155
  179.2 16.5 %collective-permute-start.11 = (f32[1,256,256]{2,1,0:T(8,128)}, f32[1,256,256]{2,1,0:T(8,128)}, u32[]{:S(2)}, u32[]{:S(2)}) collective-permute-start(f32[1,256,256]{2,1,0:T(8,128)} %fusion.23), channel_id=1, source_target_pairs={{0,16},{8,24},{16,28},{24,20},{28,12},{20,4},{12,0},{4,8},{1,17},{... | collective-permute-start | bytes 786440 | tf_op jit(solution)/shard_map/ppermute | solution.py:155
  187.1 0.7 copy-start.6
  196.7 2.9 %collective-permute-start.12 = (f32[2,512,256]{2,1,0:T(8,128)S(1)}, f32[2,512,256]{2,1,0:T(8,128)}, u32[]{:S(2)}, u32[]{:S(2)}) collective-permute-start(f32[2,512,256]{2,1,0:T(8,128)S(1)} %dynamic-slice_bitcast_fusion), channel_id=1, source_target_pairs={{0,1},{1,0},{2,3},{3,2},{4,5},{5,4},{6,7},{7,6},{8,9},{9,8},{10,11... | collective-permute-start | bytes 3145736 | tf_op jit(solution)/shard_map/ppermute | solution.py:63
  201.0 14.0 %collective-permute-start.13 = (f32[512,256]{1,0:T(8,128)S(1)}, f32[512,256]{1,0:T(8,128)S(1)}, u32[]{:S(2)}, u32[]{:S(2)}) collective-permute-start(f32[512,256]{1,0:T(8,128)S(1)} %dynamic-slice_bitcast_fusion.1), channel_id=1, source_target_pairs={{0,2},{1,3},{2,0},{3,1},{4,6},{5,7},{6,4},{7,5},{8,10},{9,11},{10,... | collective-permute-start | bytes 1572872 | tf_op jit(solution)/shard_map/ppermute | solution.py:63
